TPU v7x, 256 devices: a whole 4x4x8 slice. The times are simulated.
256 devices in a mesh: dp: 32 (over x, y, z_lo), tensor: 8 (over z_hi, core).
Axes of the slice: x: 4, y: 4, z: 8 (z_hi: 4, z_lo: 2; z = z_hi * 2 + z_lo), core: 2. Of those that a mesh axis runs over, the one named last changes fastest.
Arguments:
- arrivals: bfloat16 [32768, 2048], P('dp', 'tensor')
- deal: int32 [32, 32], P('dp'), may hold values from 0 to 1023, as said below
- seg_ids: int32 [32, 1024], P('dp'), may hold values from 0 to 7, never falling along the last dimension, each value on 1 to 512 neighbouring positions
- page_table: int32 [32, 8], P('dp'), may hold values from 0 to 7, each once within a row
- attn_gain: float32 [2048], replicated, may hold values from 0.1 to 1.9
- w_query: bfloat16 [2048, 1024], P(None, 'tensor'), may hold values from -0.125 to 0.125
- w_keyval: bfloat16 [2048, 512], replicated, may hold values from -0.125 to 0.125
- query_gain: float32 [64], replicated, may hold values from 0.1 to 1.9
- key_gain: float32 [64], replicated, may hold values from 0.1 to 1.9
- w_out: bfloat16 [1024, 2048], P('tensor'), may hold values from -0.1875 to 0.1875
- ffn_gain: float32 [2048], replicated, may hold values from 0.1 to 1.9
- w_gate: bfloat16 [2048, 5120], P(None, 'tensor'), may hold values from -0.125 to 0.125
- w_up: bfloat16 [2048, 5120], P(None, 'tensor'), may hold values from -0.125 to 0.125
- w_down: bfloat16 [5120, 2048], P('tensor'), may hold values from -0.078125 to 0.078125
Outputs:
- result: bfloat16 [32768, 2048], P('dp', 'tensor')
- kv_pages: bfloat16 [256, 128, 512], P('dp', None, 'tensor')
Inputs may be any that keep to these rules, and one draw needn't show every extreme that they name: deal[s, k] = g * 32 + j sends unit k of arrival block s to unit j of group g; every value occurs once; the units of one arrival block go to exactly 16 groups, 2 units to each. `seg_ids`: each row never falls; one prompt is one run of equal numbers. `page_table`: each row holds every page number once.
All inputs are finite; a program needn't handle non-finite values.
Results may differ from a plain program's by a relative error of at most 0.019.
Values may be sent and summed in bfloat16 or wider, within the bound.
No kernel may reach another device: no remote copies, remote signals or barrier semaphores. Data moves between devices by JAX's collectives and lax.ppermute only.
A program may use at most 128 MiB of HBM per device.

v0:
```python
import math
import jax
import jax.numpy as jnp
from jax import lax
from jax.sharding import PartitionSpec as P

HEAD = 64
KVH = 4
MOST = 2
PAGE = 128
EPS = 1e-06
THETA = 10000.0
BLOCK_ROWS = 512


def rms_scale(values, gain):
    values = values.astype(jnp.float32)
    mean_sq = jnp.mean(values * values, axis=-1, keepdims=True)
    return values * lax.rsqrt(mean_sq + EPS) * gain


def rope_tables(positions, width):
    half = width // 2
    inverse = THETA ** (-jnp.arange(half, dtype=jnp.float32) * 2.0 / width)
    angles = positions.astype(jnp.float32)[:, None] * inverse[None, :]
    return (jnp.cos(angles), jnp.sin(angles))


def rotate(values, cosine, sine):
    half = values.shape[-1] // 2
    first = values[..., :half]
    second = values[..., half:]
    cos_b = cosine[:, None, :]
    sin_b = sine[:, None, :]
    return jnp.concatenate(
        [first * cos_b - second * sin_b, second * cos_b + first * sin_b], axis=-1
    )


def segment_starts(seg_row):
    count = seg_row.shape[0]
    index = jnp.arange(count, dtype=jnp.int32)
    prior = jnp.concatenate([seg_row[:1] - 1, seg_row[:-1]])
    marks = jnp.where(seg_row != prior, index, 0)
    return lax.cummax(marks, axis=0)


def on_device(
    arrivals,
    deal,
    seg_ids,
    page_table,
    attn_gain,
    w_query,
    w_keyval,
    query_gain,
    key_gain,
    w_out,
    ffn_gain,
    w_gate,
    w_up,
    w_down,
):
    groups = lax.axis_size("dp")
    shards = lax.axis_size("tensor")
    tensor_rank = lax.axis_index("tensor")
    tok_grp = arrivals.shape[0]
    feat_part = arrivals.shape[1]
    units = deal.shape[1]
    unit_rows = tok_grp // units
    slot_count = groups * MOST
    width = unit_rows * feat_part
    dest_row = deal[0]
    target = dest_row // units
    position = dest_row % units
    unit_index = jnp.arange(units, dtype=jnp.int32)
    earlier = unit_index[:, None] > unit_index[None, :]
    same_target = target[:, None] == target[None, :]
    rank = jnp.sum(jnp.logical_and(earlier, same_target), axis=1)
    slot = target * MOST + rank
    send_hot = slot[None, :] == jnp.arange(slot_count, dtype=jnp.int32)[:, None]
    filled = jnp.any(send_hot, axis=1)
    slot_pos = jnp.where(filled, jnp.sum(jnp.where(send_hot, position[None, :], 0), axis=1), -1)
    send_matrix = send_hot.astype(jnp.bfloat16)
    packed = jnp.dot(
        send_matrix, arrivals.reshape(units, width), preferred_element_type=jnp.float32
    ).astype(jnp.bfloat16)
    received, recv_pos = (
        lax.all_to_all(
            packed.reshape(groups, MOST, width), "dp", split_axis=0, concat_axis=0, tiled=True
        ),
        lax.all_to_all(
            slot_pos.reshape(groups, MOST), "dp", split_axis=0, concat_axis=0, tiled=True
        ),
    )
    recv_matrix = (recv_pos.reshape(-1)[None, :] == unit_index[:, None]).astype(jnp.bfloat16)
    grouped = jnp.dot(
        recv_matrix, received.reshape(slot_count, width), preferred_element_type=jnp.float32
    ).astype(jnp.bfloat16)
    grouped = grouped.reshape(tok_grp, feat_part)
    full = lax.all_gather(grouped, "tensor", axis=1, tiled=True)
    normed = rms_scale(full, attn_gain).astype(jnp.bfloat16)
    seg_row = seg_ids[0]
    starts = segment_starts(seg_row)
    index = jnp.arange(tok_grp, dtype=jnp.int32)
    cosine, sine = rope_tables(index - starts, HEAD)
    q_heads = w_query.shape[1] // HEAD
    q_raw = jnp.dot(normed, w_query, preferred_element_type=jnp.float32).reshape(
        tok_grp, q_heads, HEAD
    )
    queries = rotate(rms_scale(q_raw, query_gain), cosine, sine).astype(jnp.bfloat16)
    kv_heads = max(1, KVH // shards)
    kv_first = tensor_rank * KVH // shards
    kv_weight = lax.dynamic_slice_in_dim(w_keyval, kv_first * 2 * HEAD, kv_heads * 2 * HEAD, 1)
    kv_raw = jnp.dot(normed, kv_weight, preferred_element_type=jnp.float32).reshape(
        tok_grp, kv_heads, 2, HEAD
    )
    keys = rotate(rms_scale(kv_raw[:, :, 0], key_gain), cosine, sine).astype(jnp.bfloat16)
    values = kv_raw[:, :, 1].astype(jnp.bfloat16)
    stacked = jnp.stack([keys, values], axis=2).reshape(tok_grp, kv_heads * 2 * HEAD)
    cache_cols = 2 * KVH * HEAD // shards
    offset = tensor_rank * cache_cols - kv_first * 2 * HEAD
    own_cache = lax.dynamic_slice_in_dim(stacked, offset, cache_cols, 1)
    pages = own_cache.reshape(tok_grp // PAGE, PAGE, cache_cols)
    kv_pages = jnp.zeros_like(pages).at[page_table[0]].set(pages)
    share = q_heads // kv_heads
    grouped_q = queries.reshape(tok_grp, kv_heads, share, HEAD)
    scale = 1.0 / math.sqrt(HEAD)
    block = min(BLOCK_ROWS, tok_grp)
    outputs = []
    for first in range(0, tok_grp, block):
        last = first + block
        scores = (
            jnp.einsum(
                "ikgd,jkd->kgij",
                grouped_q[first:last],
                keys[:last],
                preferred_element_type=jnp.float32,
            )
            * scale
        )
        query_rows = index[first:last]
        allowed = jnp.logical_and(
            query_rows[:, None] >= index[None, :last],
            starts[first:last][:, None] <= index[None, :last],
        )
        weights = jnp.where(allowed, jnp.exp(scores), 0.0)
        probs = (weights / jnp.sum(weights, axis=-1, keepdims=True)).astype(jnp.bfloat16)
        mixed = jnp.einsum(
            "kgij,jkd->ikgd", probs, values[:last], preferred_element_type=jnp.float32
        )
        outputs.append(mixed.astype(jnp.bfloat16).reshape(block, q_heads * HEAD))
    attended = jnp.concatenate(outputs, axis=0)
    attn_sum = lax.psum(
        jnp.dot(attended, w_out, preferred_element_type=jnp.float32).astype(jnp.bfloat16), "tensor"
    ).astype(jnp.float32)
    middle = (full.astype(jnp.float32) + attn_sum).astype(jnp.bfloat16)
    ffn_in = rms_scale(middle, ffn_gain).astype(jnp.bfloat16)
    gate = jnp.dot(ffn_in, w_gate, preferred_element_type=jnp.float32)
    upper = jnp.dot(ffn_in, w_up, preferred_element_type=jnp.float32)
    hidden = (jax.nn.silu(gate) * upper).astype(jnp.bfloat16)
    ffn_part = lax.psum_scatter(
        jnp.dot(hidden, w_down, preferred_element_type=jnp.float32).astype(jnp.bfloat16),
        "tensor",
        scatter_dimension=1,
        tiled=True,
    ).astype(jnp.float32)
    own_cols = lax.dynamic_slice_in_dim(middle, tensor_rank * feat_part, feat_part, 1)
    combined = (own_cols.astype(jnp.float32) + ffn_part).astype(jnp.bfloat16)
    back = jnp.dot(
        recv_matrix.T, combined.reshape(units, width), preferred_element_type=jnp.float32
    ).astype(jnp.bfloat16)
    returned = lax.all_to_all(
        back.reshape(groups, MOST, width), "dp", split_axis=0, concat_axis=0, tiled=True
    )
    result = jnp.dot(
        send_matrix.T, returned.reshape(slot_count, width), preferred_element_type=jnp.float32
    ).astype(jnp.bfloat16)
    return (result.reshape(tok_grp, feat_part), kv_pages)


def solution(mesh):
    return jax.shard_map(
        on_device,
        mesh=mesh,
        in_specs=(
            P("dp", "tensor"),
            P("dp", None),
            P("dp", None),
            P("dp", None),
            P(),
            P(None, "tensor"),
            P(),
            P(),
            P(),
            P("tensor", None),
            P(),
            P(None, "tensor"),
            P(None, "tensor"),
            P("tensor", None),
        ),
        out_specs=(P("dp", "tensor"), P("dp", None, "tensor")),
        check_vma=False,
    )
```

profile of v0, /device:TPU:65, one launch (start us, length us, event | category | flops | bytes accessed | tf_op | source)
XLA Modules:
  0.0 368.1 jit_solution(12057154090771228152)
XLA Ops:
  9.8 8.4 %all-to-all-start = ((s32[32,1,2]{2,1,0:T(1,128)}), s32[32,1,2]{2,1,0:T(1,128)S(1)}, u32[]{:S(2)}, u32[]{:S(2)}) async-start(s32[32,1,2]{2,1,0:T(1,128)} %bitcast.5), calls=%async_computation | async-start | bytes 32768 | tf_op jit(solution)/shard_map/all_to_all | solution.py:92
  18.2 1.3 reshape.501
  19.5 1.5 convolution_convert_fusion.1
  21.0 2.5 reshape.502
  23.5 1.7 all-to-all-done
  25.2 6.3 %all-to-all-start.1 = ((bf16[32,2,8192]{2,1,0:T(2,128)(2,1)}), bf16[32,2,8192]{2,1,0:T(2,128)(2,1)}, u32[]{:S(2)}, u32[]{:S(2)}) async-start(bf16[32,2,8192]{2,1,0:T(2,128)(2,1)} %reshape.502), calls=%async_computation.1 | async-start | bytes 2097152 | tf_op jit(solution)/shard_map/all_to_all | solution.py:89
  32.9 14.9 %all-to-all-done.1 = bf16[32,2,8192]{2,1,0:T(2,128)(2,1)} async-done(((bf16[32,2,8192]{2,1,0:T(2,128)(2,1)}), bf16[32,2,8192]{2,1,0:T(2,128)(2,1)}, u32[]{:S(2)}, u32[]{:S(2)}) %all-to-all-start.1) | async-done | bytes 1048608 | tf_op jit(solution)/shard_map/all_to_all | solution.py:89
  47.8 2.3 reshape.503
  50.1 1.5 convolution_convert_fusion.3
  51.6 1.0 reshape.504
  56.8 52.7 %all-gather.2.cloned.1.call-done = bf16[1024,2048]{1,0:T(8,128)(2,1)} async-done(((bf16[1024,256]{1,0:T(8,128)(2,1)}), bf16[1024,2048]{1,0:T(8,128)(2,1)}) %all-gather.2.cloned.1.call-update) | async-done | bytes 4194320 | tf_op jit(solution)/shard_map/all_gather | solution.py:101
  109.5 3.2 fusion.3
  113.0 2.6 fusion.19
  116.4 1.6 multiply_reduce_fusion
  119.0 1.1 fusion.7
  120.1 1.3 fusion.21
  122.5 3.3 convolution_convert_fusion.5
  126.0 116.0 %all-reduce.2.cloned.1.call-done = bf16[1024,2048]{1,0:T(8,128)(2,1)} async-done(((bf16[1024,2048]{1,0:T(8,128)(2,1)}), bf16[1024,2048]{1,0:T(8,128)(2,1)}) %all-reduce.2.cloned.1.call-update) | async-done | bytes 4194320 | tf_op jit(solution)/shard_map/psum | solution.py:154
  242.0 5.6 %fusion = (f32[1024]{0:T(1024)S(1)}, bf16[1024,2048]{1,0:T(8,128)(2,1)S(1)}) fusion(bf16[1024,2048]{1,0:T(8,128)(2,1)} %all-reduce.2.cloned.1.call-done, bf16[1024,2048]{1,0:T(8,128)(2,1)} %all-gather.2.cloned.1.call-done), kind=kLoop, calls=%fused_computation.10 | loop fusion | flops 14679040 | bytes 12587008 | tf_op jit(solution)/shard_map/reduce_sum | solution.py:18
  247.6 1.9 copy-done.2
  249.6 5.1 %fusion.13 = f32[1024,640]{1,0:T(8,128)} fusion(bf16[2048,640]{1,0:T(8,128)(2,1)S(1)} %copy-done.13, bf16[1024,2048]{1,0:T(8,128)(2,1)S(1)} %get-tuple-element.3, f32[2048]{0:T(1024)S(1)} %copy-done.17, f32[1024]{0:T(1024)S(1)} %add_rsqrt_fusion.1), kind=kOutput, calls=%fused_computation.31 | convolution fusion | flops 2692743168 | bytes 9449472 | tf_op jit(solution)/shard_map/dot_general | solution.py:159
  254.6 12.3 %convolution_convert_fusion.4 = bf16[1024,2048]{1,0:T(8,128)(2,1)} fusion(bf16[640,2048]{1,0:T(8,128)(2,1)S(1)} %copy-done, f32[1024,640]{1,0:T(8,128)} %fusion.13, bf16[2048,640]{1,0:T(8,128)(2,1)} %param.26, bf16[1024,2048]{1,0:T(8,128)(2,1)} %copy-done.2, f32[2048]{0:T(1024)S(1)} %copy-done.17, f32[1024]{0:T(1024)S(1)} %add_rsqrt_fusion.1), kind=kOutput, calls=%fused_computation.19 | convolution fusion | flops 5383127040 | bytes 16265216 | tf_op jit(solution)/shard_map/dot_general | solution.py:163
  267.0 59.3 %reduce-scatter.2.cloned.1.call-done = bf16[1024,256]{1,0:T(8,128)(2,1)} async-done(((bf16[1024,2048]{1,0:T(8,128)(2,1)}), bf16[1024,256]{1,0:T(8,128)(2,1)}) %reduce-scatter.2.cloned.1.call-update) | async-done | bytes 524304 | tf_op jit(solution)/shard_map/reduce_scatter | solution.py:162
  326.3 1.3 add_convert_fusion
  327.6 1.0 reshape.514
  328.7 2.5 convolution_convert_fusion
  331.2 2.5 reshape.515
  333.7 6.5 %all-to-all-start.2 = ((bf16[32,2,8192]{2,1,0:T(2,128)(2,1)}), bf16[32,2,8192]{2,1,0:T(2,128)(2,1)}, u32[]{:S(2)}, u32[]{:S(2)}) async-start(bf16[32,2,8192]{2,1,0:T(2,128)(2,1)} %reshape.515), calls=%async_computation.3 | async-start | bytes 2097152 | tf_op jit(solution)/shard_map/all_to_all | solution.py:173
  341.2 15.5 %all-to-all-done.2 = bf16[32,2,8192]{2,1,0:T(2,128)(2,1)} async-done(((bf16[32,2,8192]{2,1,0:T(2,128)(2,1)}), bf16[32,2,8192]{2,1,0:T(2,128)(2,1)}, u32[]{:S(2)}, u32[]{:S(2)}) %all-to-all-start.2) | async-done | bytes 1048608 | tf_op jit(solution)/shard_map/all_to_all | solution.py:173
  356.6 2.3 reshape.516
  358.9 1.6 convolution_convert_fusion.2
  360.5 1.0 reshape.517
  (87 shorter events, 11.5 us)
Async XLA Ops:
  7.2 247.5 %copy-start = (bf16[640,2048]{1,0:T(8,128)(2,1)S(1)}, bf16[640,2048]{1,0:T(8,128)(2,1)}, u32[]{:S(2)}) copy-start(bf16[640,2048]{1,0:T(8,128)(2,1)} %param.27) | copy-start | bytes 7864324
  9.8 15.4 %all-to-all-start = ((s32[32,1,2]{2,1,0:T(1,128)}), s32[32,1,2]{2,1,0:T(1,128)S(1)}, u32[]{:S(2)}, u32[]{:S(2)}) async-start(s32[32,1,2]{2,1,0:T(1,128)} %bitcast.5), calls=%async_computation | async-start | bytes 32768 | tf_op jit(solution)/shard_map/all_to_all | solution.py:92
  23.5 29.4 %copy-start.10 = (s32[1,1024]{1,0:T(1,128)S(1)}, s32[1,1024]{1,0:T(1,128)}, u32[]{:S(2)}) copy-start(s32[1,1024]{1,0:T(1,128)} %param.16) | copy-start | bytes 12292
  25.2 22.6 %all-to-all-start.1 = ((bf16[32,2,8192]{2,1,0:T(2,128)(2,1)}), bf16[32,2,8192]{2,1,0:T(2,128)(2,1)}, u32[]{:S(2)}, u32[]{:S(2)}) async-start(bf16[32,2,8192]{2,1,0:T(2,128)(2,1)} %reshape.502), calls=%async_computation.1 | async-start | bytes 2097152 | tf_op jit(solution)/shard_map/all_to_all | solution.py:89
  31.5 78.0 %all-gather.2.cloned.1.call-start = ((), (), s32[]{:S(2)}) async-start(), calls=%async_computation.4 | async-start | bytes 4718592 | tf_op jit(solution)/shard_map/all_gather | solution.py:101
  50.1 62.7 %copy-start.15 = (f32[2048]{0:T(1024)S(1)}, f32[2048]{0:T(1024)}, u32[]{:S(2)}) copy-start(f32[2048]{0:T(1024)} %param.18) | copy-start | bytes 24580
  52.6 189.4 %all-reduce.2.cloned.1.call-start = ((), (), s32[]{:S(2)}) async-start(), calls=%async_computation.5 | async-start | bytes 8388608 | tf_op jit(solution)/shard_map/psum | solution.py:154
  109.5 3.4 copy-start.1
  113.0 2.7 copy-start.11
  113.0 3.4 copy-start.14
  113.0 3.4 copy-start.16
  116.4 2.6 copy-start.6
  116.4 2.6 copy-start.8
  116.4 1.6 copy-start.12
  116.4 1.8 copy-start.5
  121.4 1.0 copy-start.4
  125.8 123.8 %copy-start.17 = (f32[2048]{0:T(1024)S(1)}, f32[2048]{0:T(1024)}, u32[]{:S(2)}) copy-start(f32[2048]{0:T(1024)} %param.24) | copy-start | bytes 24580
  125.8 200.5 %reduce-scatter.2.cloned.1.call-start = ((), (), s32[]{:S(2)}) async-start(), calls=%async_computation.6 | async-start | bytes 4718592 | tf_op jit(solution)/shard_map/reduce_scatter | solution.py:162
  242.0 7.5 %copy-start.13 = (bf16[2048,640]{1,0:T(8,128)(2,1)S(1)}, bf16[2048,640]{1,0:T(8,128)(2,1)}, u32[]{:S(2)}) copy-start(bf16[2048,640]{1,0:T(8,128)(2,1)} %param.25) | copy-start | bytes 7864324
  247.6 1.9 copy-start.2
  267.0 73.3 %copy-start.18 = (s32[1,8]{1,0:T(1,128)S(1)}, s32[1,8]{1,0:T(1,128)}, u32[]{:S(2)}) copy-start(s32[1,8]{1,0:T(1,128)} %param.17) | copy-start | bytes 100
  267.0 73.3 %copy-start.7 = (bf16[1024,1,32]{0,2,1:T(8,128)(2,1)S(1)}, bf16[1024,1,32]{0,2,1:T(8,128)(2,1)}, u32[]{:S(2)}) copy-start(bf16[1024,1,32]{0,2,1:T(8,128)(2,1)} %copy-done.6) | copy-start | bytes 196612
  267.0 73.3 %copy-start.9 = (bf16[1024,1,32]{0,2,1:T(8,128)(2,1)S(1)}, bf16[1024,1,32]{0,2,1:T(8,128)(2,1)}, u32[]{:S(2)}) copy-start(bf16[1024,1,32]{0,2,1:T(8,128)(2,1)} %copy-done.8) | copy-start | bytes 196612
  333.7 22.9 %all-to-all-start.2 = ((bf16[32,2,8192]{2,1,0:T(2,128)(2,1)}), bf16[32,2,8192]{2,1,0:T(2,128)(2,1)}, u32[]{:S(2)}, u32[]{:S(2)}) async-start(bf16[32,2,8192]{2,1,0:T(2,128)(2,1)} %reshape.515), calls=%async_computation.3 | async-start | bytes 2097152 | tf_op jit(solution)/shard_map/all_to_all | solution.py:173
  341.2 20.4 %copy-start.3 = (bf16[8,128,64]{1,2,0:T(8,128)(2,1)}, bf16[8,128,64]{1,2,0:T(8,128)(2,1)S(1)}, u32[]{:S(2)}) copy-start(bf16[8,128,64]{1,2,0:T(8,128)(2,1)S(1)} %scatter_fusion) | copy-start | bytes 393220
Sparse Core Ops, SparseCore 0:
  52.8 56.6 all-gather.1
  125.9 116.0 all-reduce.1
  267.1 59.1 reduce-scatter.1
where the time goes:
time: 369 us; the launch traced here: 368 us
  waiting for transfers between devices  260 us (70%)
  matrix products  35.9 us (10%)
  starting transfers between devices  21.8 us (6%)
  local copies, waits for them, and re-layouts  19.4 us (5%)
  other arithmetic  16.1 us (4%)
  between operations  14.9 us (4%)
    psum x1, waiting for transfers between devices, on_device(): lax.psum(jnp.dot(attended, w_out, preferred_element_type=jnp.float32).ast...  116 us
    reduce_scatter x1, waiting for transfers between devices, on_device(): lax.psum_scatter(jnp.dot(hidden, w_down, preferred_element_type=jnp.float...  59.3 us
    all_gather x1, waiting for transfers between devices, on_device(): full = lax.all_gather(grouped, 'tensor', axis=1, tiled=True)  52.7 us
    all_to_all x1, waiting for transfers between devices, on_device(): lax.all_to_all(back.reshape(groups, MOST, width), 'dp', split_axis=0, con...  15.5 us
    all_to_all x1, waiting for transfers between devices, on_device(): lax.all_to_all(packed.reshape(groups, MOST, width), 'dp', split_axis=0, c...  14.9 us
    dot_general x1, matrix products, on_device(): jnp.dot(hidden, w_down, preferred_element_type=jnp.float32)  12.3 us
    reduce_sum x3, other arithmetic, rms_scale(): mean_sq = jnp.mean(values * values, axis=-1, keepdims=True)  8.85 us
    all_to_all x1, starting transfers between devices, on_device(): lax.all_to_all(slot_pos.reshape(groups, MOST), 'dp', split_axis=0, concat...  8.39 us
  transfers between devices with their start and end apart: 6, of which 6 were waited for; matrix products, arithmetic and copies ran while one was open for 3% of the time, Pallas kernels for 0%

commit v1 on v0

--- a/solution.py
+++ b/solution.py
@@ -151,8 +151,12 @@
         )
         outputs.append(mixed.astype(jnp.bfloat16).reshape(block, q_heads * HEAD))
     attended = jnp.concatenate(outputs, axis=0)
-    attn_sum = lax.psum(
-        jnp.dot(attended, w_out, preferred_element_type=jnp.float32).astype(jnp.bfloat16), "tensor"
+    attn_sum = jnp.sum(
+        lax.all_gather(
+            jnp.dot(attended, w_out, preferred_element_type=jnp.float32).astype(jnp.bfloat16),
+            "tensor",
+        ),
+        axis=0,
     ).astype(jnp.float32)
     middle = (full.astype(jnp.float32) + attn_sum).astype(jnp.bfloat16)
     ffn_in = rms_scale(middle, ffn_gain).astype(jnp.bfloat16)

time: 369 us -> 560 us (1.52)
  waiting for transfers between devices: 260 us -> 437 us
  other arithmetic: 16.1 us -> 30.2 us
    all_gather x0 -> x1, waiting for transfers between devices: none -> 290 us  [on_device(): lax.all_gather(jnp.dot(attended, w_out, preferred_element_type=jnp.float3...]
    psum x1 -> x0, waiting for transfers between devices: 116 us -> none  [on_device(): lax.psum(jnp.dot(attended, w_out, preferred_element_type=jnp.float32).ast...]
    reduce_sum x0 -> x1, other arithmetic: none -> 14.1 us  [on_device(): jnp.sum(lax.all_gather(jnp.dot(attended, w_out, preferred_element_type=jn...]
  transfers between devices with their start and end apart: 6 -> 6, of which waited for: 6 -> 6; matrix products, arithmetic and copies ran while one was open for 3% -> 2% of each run, Pallas kernels for 0% -> 0%
where the time goes in v1:
time: 560 us
  waiting for transfers between devices  437 us (78%)
  matrix products  35.9 us (6%)
  other arithmetic  30.2 us (5%)
  starting transfers between devices  21.9 us (4%)
  local copies, waits for them, and re-layouts  19.4 us (3%)
  between operations  14.9 us (3%)
    all_gather x1, waiting for transfers between devices, on_device(): lax.all_gather(jnp.dot(attended, w_out, preferred_element_type=jnp.float3...  290 us
    reduce_scatter x1, waiting for transfers between devices, on_device(): lax.psum_scatter(jnp.dot(hidden, w_down, preferred_element_type=jnp.float...  62.6 us
    all_gather x1, waiting for transfers between devices, on_device(): full = lax.all_gather(grouped, 'tensor', axis=1, tiled=True)  52.7 us
    all_to_all x1, waiting for transfers between devices, on_device(): lax.all_to_all(back.reshape(groups, MOST, width), 'dp', split_axis=0, con...  15.5 us
    all_to_all x1, waiting for transfers between devices, on_device(): lax.all_to_all(packed.reshape(groups, MOST, width), 'dp', split_axis=0, c...  14.9 us
    reduce_sum x1, other arithmetic, on_device(): jnp.sum(lax.all_gather(jnp.dot(attended, w_out, preferred_element_type=jn...  14.1 us
    dot_general x1, matrix products, on_device(): jnp.dot(hidden, w_down, preferred_element_type=jnp.float32)  12.3 us
  transfers between devices with their start and end apart: 6, of which 6 were waited for; matrix products, arithmetic and copies ran while one was open for 2% of the time, Pallas kernels for 0%

profile of v1, /device:TPU:65, one launch (start us, length us, event | category | flops | bytes accessed | tf_op | source)
XLA Modules:
  0.0 559.6 jit_solution(12280431330435254490)
XLA Ops:
  9.8 8.4 %all-to-all-start = ((s32[32,1,2]{2,1,0:T(1,128)}), s32[32,1,2]{2,1,0:T(1,128)S(1)}, u32[]{:S(2)}, u32[]{:S(2)}) async-start(s32[32,1,2]{2,1,0:T(1,128)} %bitcast.5), calls=%async_computation | async-start | bytes 32768 | tf_op jit(solution)/shard_map/all_to_all | solution.py:92
  18.2 1.3 reshape.501
  19.5 1.5 convolution_convert_fusion.1
  21.0 2.5 reshape.502
  23.5 1.7 all-to-all-done
  25.2 6.3 %all-to-all-start.1 = ((bf16[32,2,8192]{2,1,0:T(2,128)(2,1)}), bf16[32,2,8192]{2,1,0:T(2,128)(2,1)}, u32[]{:S(2)}, u32[]{:S(2)}) async-start(bf16[32,2,8192]{2,1,0:T(2,128)(2,1)} %reshape.502), calls=%async_computation.1 | async-start | bytes 2097152 | tf_op jit(solution)/shard_map/all_to_all | solution.py:89
  32.9 14.9 %all-to-all-done.1 = bf16[32,2,8192]{2,1,0:T(2,128)(2,1)} async-done(((bf16[32,2,8192]{2,1,0:T(2,128)(2,1)}), bf16[32,2,8192]{2,1,0:T(2,128)(2,1)}, u32[]{:S(2)}, u32[]{:S(2)}) %all-to-all-start.1) | async-done | bytes 1048608 | tf_op jit(solution)/shard_map/all_to_all | solution.py:89
  47.8 2.3 reshape.503
  50.1 1.5 convolution_convert_fusion.3
  51.6 1.0 reshape.504
  56.8 52.7 %all-gather.4.cloned.1.call-done = bf16[1024,2048]{1,0:T(8,128)(2,1)} async-done(((bf16[1024,256]{1,0:T(8,128)(2,1)}), bf16[1024,2048]{1,0:T(8,128)(2,1)}) %all-gather.4.cloned.1.call-update) | async-done | bytes 4194320 | tf_op jit(solution)/shard_map/all_gather | solution.py:101
  109.5 3.2 fusion.3
  113.0 2.6 fusion.19
  116.4 1.6 multiply_reduce_fusion
  119.0 1.1 fusion.7
  120.1 1.3 fusion.21
  122.5 3.2 convolution_convert_fusion.5
  126.0 290.0 %all-gather.6.cloned.1.call-done = bf16[8192,2048]{1,0:T(8,128)(2,1)} async-done(((bf16[1024,2048]{1,0:T(8,128)(2,1)}), bf16[8192,2048]{1,0:T(8,128)(2,1)}) %all-gather.6.cloned.1.call-update) | async-done | bytes 33554448 | tf_op jit(solution)/shard_map/all_gather | solution.py:155
  416.0 14.1 %reduce_sum.94 = bf16[1024,2048]{1,0:T(8,128)(2,1)} reduce(bf16[8,1024,2048]{2,1,0:T(8,128)(2,1)} %bitcast.134, bf16[]{:T(256)} %constant.101.clone.1), dimensions={0}, to_apply=%region_10.11 | reduce | flops 14680064 | bytes 37748736 | tf_op jit(solution)/shard_map/reduce_sum | solution.py:154
  430.1 5.6 %fusion = (f32[1024]{0:T(1024)S(1)}, bf16[1024,2048]{1,0:T(8,128)(2,1)S(1)}) fusion(bf16[1024,2048]{1,0:T(8,128)(2,1)} %reduce_sum.94, bf16[1024,2048]{1,0:T(8,128)(2,1)} %all-gather.4.cloned.1.call-done), kind=kLoop, calls=%fused_computation.10 | loop fusion | flops 14679040 | bytes 12587008 | tf_op jit(solution)/shard_map/reduce_sum | solution.py:18
  435.7 1.9 copy-done.2
  437.6 5.1 fusion.13
  442.7 12.3 %convolution_convert_fusion.4 = bf16[1024,2048]{1,0:T(8,128)(2,1)} fusion(bf16[640,2048]{1,0:T(8,128)(2,1)S(1)} %copy-done, f32[1024,640]{1,0:T(8,128)} %fusion.13, bf16[2048,640]{1,0:T(8,128)(2,1)} %param.26, bf16[1024,2048]{1,0:T(8,128)(2,1)} %copy-done.2, f32[2048]{0:T(1024)S(1)} %copy-done.17, f32[1024]{0:T(1024)S(1)} %add_rsqrt_fusion.1), kind=kOutput, calls=%fused_computation.19 | convolution fusion | flops 5383127040 | bytes 16265216 | tf_op jit(solution)/shard_map/dot_general | solution.py:167
  455.1 62.6 %reduce-scatter.2.cloned.1.call-done = bf16[1024,256]{1,0:T(8,128)(2,1)} async-done(((bf16[1024,2048]{1,0:T(8,128)(2,1)}), bf16[1024,256]{1,0:T(8,128)(2,1)}) %reduce-scatter.2.cloned.1.call-update) | async-done | bytes 524304 | tf_op jit(solution)/shard_map/reduce_scatter | solution.py:166
  517.8 1.3 add_convert_fusion
  519.1 1.0 reshape.514
  520.1 2.5 convolution_convert_fusion
  522.7 2.5 reshape.515
  525.2 6.6 %all-to-all-start.2 = ((bf16[32,2,8192]{2,1,0:T(2,128)(2,1)}), bf16[32,2,8192]{2,1,0:T(2,128)(2,1)}, u32[]{:S(2)}, u32[]{:S(2)}) async-start(bf16[32,2,8192]{2,1,0:T(2,128)(2,1)} %reshape.515), calls=%async_computation.3 | async-start | bytes 2097152 | tf_op jit(solution)/shard_map/all_to_all | solution.py:177
  532.8 15.5 %all-to-all-done.2 = bf16[32,2,8192]{2,1,0:T(2,128)(2,1)} async-done(((bf16[32,2,8192]{2,1,0:T(2,128)(2,1)}), bf16[32,2,8192]{2,1,0:T(2,128)(2,1)}, u32[]{:S(2)}, u32[]{:S(2)}) %all-to-all-start.2) | async-done | bytes 1048608 | tf_op jit(solution)/shard_map/all_to_all | solution.py:177
  548.2 2.3 reshape.516
  550.5 1.6 convolution_convert_fusion.2
  (88 shorter events, 12.5 us)
Async XLA Ops:
  7.2 435.6 %copy-start = (bf16[640,2048]{1,0:T(8,128)(2,1)S(1)}, bf16[640,2048]{1,0:T(8,128)(2,1)}, u32[]{:S(2)}) copy-start(bf16[640,2048]{1,0:T(8,128)(2,1)} %param.27) | copy-start | bytes 7864324
  9.8 15.4 %all-to-all-start = ((s32[32,1,2]{2,1,0:T(1,128)}), s32[32,1,2]{2,1,0:T(1,128)S(1)}, u32[]{:S(2)}, u32[]{:S(2)}) async-start(s32[32,1,2]{2,1,0:T(1,128)} %bitcast.5), calls=%async_computation | async-start | bytes 32768 | tf_op jit(solution)/shard_map/all_to_all | solution.py:92
  23.5 29.4 %copy-start.10 = (s32[1,1024]{1,0:T(1,128)S(1)}, s32[1,1024]{1,0:T(1,128)}, u32[]{:S(2)}) copy-start(s32[1,1024]{1,0:T(1,128)} %param.16) | copy-start | bytes 12292
  25.2 22.6 %all-to-all-start.1 = ((bf16[32,2,8192]{2,1,0:T(2,128)(2,1)}), bf16[32,2,8192]{2,1,0:T(2,128)(2,1)}, u32[]{:S(2)}, u32[]{:S(2)}) async-start(bf16[32,2,8192]{2,1,0:T(2,128)(2,1)} %reshape.502), calls=%async_computation.1 | async-start | bytes 2097152 | tf_op jit(solution)/shard_map/all_to_all | solution.py:89
  31.5 78.0 %all-gather.4.cloned.1.call-start = ((), (), s32[]{:S(2)}) async-start(), calls=%async_computation.4 | async-start | bytes 4718592 | tf_op jit(solution)/shard_map/all_gather | solution.py:101
  50.1 62.7 %copy-start.15 = (f32[2048]{0:T(1024)S(1)}, f32[2048]{0:T(1024)}, u32[]{:S(2)}) copy-start(f32[2048]{0:T(1024)} %param.18) | copy-start | bytes 24580
  52.6 363.3 %all-gather.6.cloned.1.call-start = ((), (), s32[]{:S(2)}) async-start(), calls=%async_computation.6 | async-start | bytes 37748736 | tf_op jit(solution)/shard_map/all_gather | solution.py:155
  109.5 3.4 copy-start.1
  113.0 2.7 copy-start.11
  113.0 3.4 copy-start.14
  113.0 3.4 copy-start.16
  116.4 2.6 copy-start.6
  116.4 2.6 copy-start.8
  116.4 1.6 copy-start.12
  116.4 1.8 copy-start.5
  121.4 1.0 copy-start.4
  125.7 392.1 %reduce-scatter.2.cloned.1.call-start = ((), (), s32[]{:S(2)}) async-start(), calls=%async_computation.5 | async-start | bytes 4718592 | tf_op jit(solution)/shard_map/reduce_scatter | solution.py:166
  430.1 7.5 %copy-start.13 = (bf16[2048,640]{1,0:T(8,128)(2,1)S(1)}, bf16[2048,640]{1,0:T(8,128)(2,1)}, u32[]{:S(2)}) copy-start(bf16[2048,640]{1,0:T(8,128)(2,1)} %param.25) | copy-start | bytes 7864324
  430.1 7.5 %copy-start.17 = (f32[2048]{0:T(1024)S(1)}, f32[2048]{0:T(1024)}, u32[]{:S(2)}) copy-start(f32[2048]{0:T(1024)} %param.24) | copy-start | bytes 24580
  435.7 1.9 copy-start.2
  455.1 76.8 %copy-start.18 = (s32[1,8]{1,0:T(1,128)S(1)}, s32[1,8]{1,0:T(1,128)}, u32[]{:S(2)}) copy-start(s32[1,8]{1,0:T(1,128)} %param.17) | copy-start | bytes 100
  455.1 76.8 %copy-start.7 = (bf16[1024,1,32]{0,2,1:T(8,128)(2,1)S(1)}, bf16[1024,1,32]{0,2,1:T(8,128)(2,1)}, u32[]{:S(2)}) copy-start(bf16[1024,1,32]{0,2,1:T(8,128)(2,1)} %copy-done.6) | copy-start | bytes 196612
  455.1 76.8 %copy-start.9 = (bf16[1024,1,32]{0,2,1:T(8,128)(2,1)S(1)}, bf16[1024,1,32]{0,2,1:T(8,128)(2,1)}, u32[]{:S(2)}) copy-start(bf16[1024,1,32]{0,2,1:T(8,128)(2,1)} %copy-done.8) | copy-start | bytes 196612
  525.2 23.0 %all-to-all-start.2 = ((bf16[32,2,8192]{2,1,0:T(2,128)(2,1)}), bf16[32,2,8192]{2,1,0:T(2,128)(2,1)}, u32[]{:S(2)}, u32[]{:S(2)}) async-start(bf16[32,2,8192]{2,1,0:T(2,128)(2,1)} %reshape.515), calls=%async_computation.3 | async-start | bytes 2097152 | tf_op jit(solution)/shard_map/all_to_all | solution.py:177
  532.8 20.4 %copy-start.3 = (bf16[8,128,64]{1,2,0:T(8,128)(2,1)}, bf16[8,128,64]{1,2,0:T(8,128)(2,1)S(1)}, u32[]{:S(2)}) copy-start(bf16[8,128,64]{1,2,0:T(8,128)(2,1)S(1)} %scatter_fusion) | copy-start | bytes 393220
Sparse Core Ops, SparseCore 0:
  52.8 56.6 all-gather.3
  125.8 290.0 all-gather.5
  455.2 62.5 reduce-scatter.1
